TPU v7x, 32 devices: a whole 2x2x4 slice. The times are simulated.
32 devices in a mesh: seq: 8 (over z, y), head: 4 (over x, core).
Axes of the slice: x: 2, y: 2, z: 4, core: 2. Of those that a mesh axis runs over, the one named last changes fastest.
Arguments:
- projected: bfloat16 [1024, 3, 4096], P('seq', None, 'head'), may hold values from -8 to 8
- destination: int32 [1024], P('seq'), may hold values from 0 to 1023, as said below
- doc_lengths: int32 [4], replicated, may hold values from 1 to 512, 1024 in all
- random_blocks: int32 [8, 3], replicated, may hold values from 0 to 7, as said below
- global_owner: int32 [8], replicated, may hold values from 0 to 7, as said below
- out_weight: bfloat16 [4096, 4096], P('head'), may hold values from -0.09375 to 0.09375
Outputs:
- attended: bfloat16 [1024, 4096], P(('seq', 'head'))
Inputs may be any that keep to these rules, and one draw needn't show every extreme that they name: Each packed position appears exactly once. Of the rows of one device (one index of seq, 128 rows), at most 32 have destinations owned by one owner (destination // 128), and in every draw some device sends exactly 32 rows to some owner. The owner (index) of random_blocks[b, r] lies at most 2 owners away from the owner of block b, counted cyclically over the owners. `global_owner`: each owner appears exactly once.
All inputs are finite; a program needn't handle non-finite values.
Results may differ from a plain program's by a relative error of at most 0.015.
Values may be sent and summed in bfloat16 or wider, within the bound.
No kernel may reach another device: no remote copies, remote signals or barrier semaphores. Data moves between devices by JAX's collectives and lax.ppermute only.
A program may use at most 128 MiB of HBM per device.

v0:
```python
import math
import jax
import jax.numpy as jnp
from jax import lax
from jax.sharding import PartitionSpec as P

HD = 128
BLK = 128
R = 3
RDEV = 2
big_negative = -1e30


def from_behind(block, axis, distance):
    devices = range(lax.axis_size(axis))
    route = [((i - distance) % len(devices), i) for i in devices]
    return lax.ppermute(block, axis, route)


def from_root(x, axis, root):
    mine = lax.axis_index(axis) == root
    return lax.psum(jnp.where(mine, x, jnp.zeros_like(x)), axis)


def combined_all(x, axis, combine):
    everything = jax.tree.map(lambda part: lax.all_gather(part, axis), x)
    first = jax.tree.map(lambda part: part[0], everything)

    def step(k, so_far):
        return combine(so_far, jax.tree.map(lambda part: part[k], everything))

    return lax.fori_loop(1, lax.axis_size(axis), step, first)


def segment_of(positions, bounds):
    return jnp.sum((bounds[None, :] <= positions[:, None]).astype(jnp.int32), axis=1)


def combine_parts(left_part, right_part):
    top_left, total_left, accum_left = left_part
    top_right, total_right, accum_right = right_part
    row_peak = jnp.maximum(top_left, top_right)
    factor_left = jnp.exp(top_left - row_peak)
    factor_right = jnp.exp(top_right - row_peak)
    return (
        row_peak,
        total_left * factor_left + total_right * factor_right,
        accum_left * factor_left[:, :, None] + accum_right * factor_right[:, :, None],
    )


def shards_ring(projected, destination, doc_lengths, random_blocks, global_owner, out_weight):
    owners = lax.axis_size("seq")
    own_index = lax.axis_index("seq")
    tok_dev = projected.shape[0]
    columns = projected.shape[2]
    heads_here = columns // HD
    per_dev = tok_dev // BLK
    blocks_all = owners * per_dev
    capacity = 2 * (tok_dev // owners)
    score_scale = 1.0 / math.sqrt(HD)
    target_owner = destination // tok_dev
    onehot = (target_owner[:, None] == jnp.arange(owners, dtype=jnp.int32)[None, :]).astype(
        jnp.int32
    )
    before = jnp.cumsum(onehot, axis=0) - onehot
    slot_rank = jnp.sum(before * onehot, axis=1)
    outgoing = (
        jnp.zeros((owners, capacity, 3, columns), projected.dtype)
        .at[target_owner, slot_rank]
        .set(projected)
    )
    slots = (
        jnp.full((owners, capacity), -1, jnp.int32)
        .at[target_owner, slot_rank]
        .set(destination % tok_dev)
    )
    incoming, landing = (
        lax.all_to_all(outgoing, "seq", split_axis=0, concat_axis=0, tiled=True),
        lax.all_to_all(slots, "seq", split_axis=0, concat_axis=0, tiled=True),
    )
    landing = landing.reshape(-1)
    landing = jnp.where(landing >= 0, landing, tok_dev)
    routed = (
        jnp.zeros((tok_dev, 3, columns), projected.dtype)
        .at[landing]
        .set(incoming.reshape(owners * capacity, 3, columns), mode="drop")
    )
    keyval = routed[:, 1:, :]
    fetched = {0: keyval}
    offsets = list(range(-RDEV, 0)) + list(range(1, RDEV + 1))
    for offset in offsets:
        fetched[offset] = from_behind(keyval, "seq", -offset)
    band_blocks = jnp.stack([fetched[offset] for offset in range(-RDEV, RDEV + 1)])
    block_ids = own_index * per_dev + jnp.arange(per_dev, dtype=jnp.int32)
    local_pick = jnp.arange(per_dev, dtype=jnp.int32) + RDEV * per_dev
    window_pick = local_pick[:, None] + jnp.arange(-1, 2, dtype=jnp.int32)[None, :]
    chosen_rand = lax.dynamic_slice_in_dim(random_blocks, own_index * per_dev, per_dev, 0)
    away_dev = (chosen_rand // per_dev - own_index) % owners
    away_dev = jnp.where(away_dev > owners // 2, away_dev - owners, away_dev)
    rand_pick = (away_dev + RDEV) * per_dev + chosen_rand % per_dev
    block_picks = jnp.concatenate([window_pick, rand_pick], axis=1)
    gathered = jnp.take(band_blocks, block_picks, axis=0)
    near_keys = gathered[:, :, :, 0, :].reshape(per_dev, (3 + R) * BLK, heads_here, HD)
    near_values = gathered[:, :, :, 1, :].reshape(per_dev, (3 + R) * BLK, heads_here, HD)
    owner_dev = global_owner[0]
    global_rows = from_root(routed, "seq", owner_dev)
    glob_keys = global_rows[:, 1, :].reshape(tok_dev, heads_here, HD)
    glob_values = global_rows[:, 2, :].reshape(tok_dev, heads_here, HD)
    queries = routed[:, 0, :].reshape(per_dev, BLK, heads_here, HD)
    near_scores = (
        jnp.einsum("bqhd,bkhd->bhqk", queries, near_keys, preferred_element_type=jnp.float32)
        * score_scale
    )
    far_scores = (
        jnp.einsum("bqhd,khd->bhqk", queries, glob_keys, preferred_element_type=jnp.float32)
        * score_scale
    )
    bounds = jnp.cumsum(doc_lengths)
    query_pos = own_index * tok_dev + jnp.arange(tok_dev, dtype=jnp.int32)
    query_doc = segment_of(query_pos, bounds).reshape(per_dev, BLK)
    window_blocks = (block_ids[:, None] + jnp.arange(-1, 2, dtype=jnp.int32)[None, :]) % blocks_all
    key_pos = (
        window_blocks[:, :, None] * BLK + jnp.arange(BLK, dtype=jnp.int32)[None, None, :]
    ).reshape(-1)
    key_doc = segment_of(key_pos, bounds).reshape(per_dev, 3 * BLK)
    same_doc = query_doc[:, :, None] == key_doc[:, None, :]
    allowed = jnp.concatenate(
        [same_doc, jnp.ones((per_dev, BLK, R * BLK), dtype=jnp.bool_)], axis=2
    )
    near_scores = jnp.where(allowed[:, None], near_scores, big_negative)
    row_peak = jnp.maximum(jnp.max(near_scores, axis=3), jnp.max(far_scores, axis=3))
    near_exp = jnp.exp(near_scores - row_peak[..., None])
    far_exp = jnp.exp(far_scores - row_peak[..., None])
    denominator = jnp.sum(near_exp, axis=3) + jnp.sum(far_exp, axis=3)
    mixed_sum = jnp.einsum(
        "bhqk,bkhd->bqhd",
        near_exp.astype(jnp.bfloat16),
        near_values,
        preferred_element_type=jnp.float32,
    )
    mixed_sum = mixed_sum + jnp.einsum(
        "bhqk,khd->bqhd",
        far_exp.astype(jnp.bfloat16),
        glob_values,
        preferred_element_type=jnp.float32,
    )
    sparse = (mixed_sum / jnp.transpose(denominator, (0, 2, 1))[..., None]).reshape(
        tok_dev, columns
    )
    sparse = sparse.astype(jnp.bfloat16)
    glob_queries = global_rows[:, 0, :].reshape(tok_dev, heads_here, HD)
    local_keys = routed[:, 1, :].reshape(tok_dev, heads_here, HD)
    local_values = routed[:, 2, :].reshape(tok_dev, heads_here, HD).astype(jnp.float32)
    all_scores = (
        jnp.einsum("qhd,khd->hqk", glob_queries, local_keys, preferred_element_type=jnp.float32)
        * score_scale
    )
    local_peak = jnp.max(all_scores, axis=2)
    weights = jnp.exp(all_scores - local_peak[..., None])
    part_total = jnp.sum(weights, axis=2)
    part_accum = jnp.einsum("hqk,khd->hqd", weights, local_values, precision=lax.Precision.HIGHEST)
    peak_all, total_all, accum_all = combined_all(
        (local_peak, part_total, part_accum), "seq", combine_parts
    )
    glob_out = jnp.transpose(accum_all / total_all[..., None], (1, 0, 2)).reshape(tok_dev, columns)
    glob_out = glob_out.astype(jnp.bfloat16)
    attn_rows = jnp.where(own_index == owner_dev, glob_out, sparse)
    return lax.psum_scatter(
        jnp.dot(attn_rows, out_weight, preferred_element_type=jnp.float32).astype(jnp.bfloat16),
        "head",
        scatter_dimension=0,
        tiled=True,
    )


def gathered_plan(projected, destination, doc_lengths, random_blocks, global_owner, out_weight):
    owners = lax.axis_size("seq")
    own_index = lax.axis_index("seq")
    tok_dev = projected.shape[0]
    columns = projected.shape[2]
    heads_here = columns // HD
    tokens = owners * tok_dev
    blocks_all = tokens // BLK
    score_scale = 1.0 / math.sqrt(HD)
    everything = lax.all_gather(projected, "seq", tiled=True)
    arrival_dest = lax.all_gather(destination, "seq", tiled=True)
    my_pos = own_index * tok_dev + jnp.arange(tok_dev, dtype=jnp.int32)
    pick = (arrival_dest[None, :] == my_pos[:, None]).astype(projected.dtype)
    queries = jnp.dot(pick, everything[:, 0, :], preferred_element_type=jnp.float32)
    queries = queries.astype(projected.dtype).reshape(tok_dev, heads_here, HD)
    keys = everything[:, 1, :].reshape(tokens, heads_here, HD)
    values = everything[:, 2, :].reshape(tokens, heads_here, HD)
    scores = (
        jnp.einsum("qhd,khd->hqk", queries, keys, preferred_element_type=jnp.float32) * score_scale
    )
    bounds = jnp.cumsum(doc_lengths)
    key_block = arrival_dest // BLK
    key_doc = segment_of(arrival_dest, bounds)
    query_block = my_pos // BLK
    query_doc = segment_of(my_pos, bounds)
    same_doc = query_doc[:, None] == key_doc[None, :]
    window = jnp.zeros((tok_dev, tokens), jnp.int32)
    for step in (-1, 0, 1):
        near = (query_block + step) % blocks_all
        window = window + (key_block[None, :] == near[:, None]).astype(jnp.int32)
    window = jnp.where(same_doc, window, 0)
    chosen = random_blocks[query_block]
    drawn = jnp.zeros((tok_dev, tokens), jnp.int32)
    for r in range(chosen.shape[1]):
        drawn = drawn + (key_block[None, :] == chosen[:, r][:, None]).astype(jnp.int32)
    glob_start = global_owner[0] * tok_dev
    in_glob = (arrival_dest >= glob_start) & (arrival_dest < glob_start + tok_dev)
    count = window + drawn + in_glob[None, :].astype(jnp.int32)
    live = count > 0
    near_scores = jnp.where(live[None], scores, big_negative)
    row_peak = jnp.max(near_scores, axis=2)
    near_exp = jnp.exp(near_scores - row_peak[..., None])
    count_f = count.astype(jnp.float32)[None]
    denominator = jnp.sum(near_exp * count_f, axis=2)
    weighted = near_exp.astype(jnp.bfloat16).astype(jnp.float32) * count_f
    weight_hi = weighted.astype(jnp.bfloat16)
    weight_lo = (weighted - weight_hi.astype(jnp.float32)).astype(jnp.bfloat16)
    mixed_sum = jnp.einsum("hqk,khd->qhd", weight_hi, values, preferred_element_type=jnp.float32)
    mixed_sum = mixed_sum + jnp.einsum(
        "hqk,khd->qhd", weight_lo, values, preferred_element_type=jnp.float32
    )
    sparse = (mixed_sum / jnp.transpose(denominator)[..., None]).reshape(tok_dev, columns)
    sparse = sparse.astype(jnp.bfloat16)
    glob_peak = jnp.max(scores, axis=2)
    glob_exp = jnp.exp(scores - glob_peak[..., None])
    glob_total = jnp.sum(glob_exp, axis=2)
    glob_accum = jnp.einsum(
        "hqk,khd->qhd", glob_exp, values.astype(jnp.float32), precision=lax.Precision.HIGHEST
    )
    glob_out = (glob_accum / jnp.transpose(glob_total)[..., None]).reshape(tok_dev, columns)
    glob_out = glob_out.astype(jnp.bfloat16)
    attn_rows = jnp.where(own_index == global_owner[0], glob_out, sparse)
    return lax.psum_scatter(
        jnp.dot(attn_rows, out_weight, preferred_element_type=jnp.float32).astype(jnp.bfloat16),
        "head",
        scatter_dimension=0,
        tiled=True,
    )


GATHER_LIMIT = 16 * 2**20


def shards(projected, destination, doc_lengths, random_blocks, global_owner, out_weight):
    gathered_bytes = lax.axis_size("seq") * projected.size * projected.dtype.itemsize
    if gathered_bytes <= GATHER_LIMIT:
        return gathered_plan(
            projected, destination, doc_lengths, random_blocks, global_owner, out_weight
        )
    return shards_ring(projected, destination, doc_lengths, random_blocks, global_owner, out_weight)


def solution(mesh):
    in_specs = (P("seq", None, "head"), P("seq"), P(), P(), P(), P("head", None))
    out_specs = P(("seq", "head"), None)
    return jax.shard_map(shards, mesh=mesh, in_specs=in_specs, out_specs=out_specs, check_vma=False)
```

profile of v0, /device:TPU:0, one launch (start us, length us, event | category | flops | bytes accessed | tf_op | source)
XLA Modules:
  0.0 158.5 jit_solution(2768139149473016350)
XLA Ops:
  6.5 2.3 %copy.18 = bf16[128,3,1024]{0,2,1:T(8,128)(2,1)} copy(bf16[128,3,1024]{2,0,1:T(8,128)(2,1)} %param.6) | data formatting | bytes 1572864 | tf_op args[0]
  8.9 0.0 reduce-scatter.2.cloned.1.call-start
  10.2 0.8 copy.21
  11.0 0.8 reduce-window.8
  11.8 0.6 gather_fusion
  12.5 22.5 %all-gather = s32[8,1,128]{2,1,0:T(1,128)S(1)} all-gather(s32[1,1,128]{2,1,0:T(1,128)} %bitcast.59), channel_id=1, replica_groups=mesh['seq'=8,'head'=4] {'seq'}, dimensions={0}, use_global_device_ids=true | all-gather | bytes 4608 | tf_op jit(solution)/shard_map/all_gather | solution.py:187
  35.0 0.1 convert_reduce_fusion.1
  35.1 0.1 convert_reduce_fusion
  35.2 0.2 slice_reduce_fusion.2
  35.4 0.5 fusion.34
  35.9 0.5 fusion.33
  36.4 75.7 %all-gather.3.cloned.1.call-done = bf16[1024,3,1024]{0,2,1:T(8,128)(2,1)} async-done(((bf16[128,3,1024]{0,2,1:T(8,128)(2,1)}), bf16[1024,3,1024]{0,2,1:T(8,128)(2,1)}) %all-gather.3.cloned.1.call-update) | async-done | bytes 6291472 | tf_op jit(solution)/shard_map/all_gather | solution.py:186
  112.1 2.7 %fusion.49 = (bf16[1024,1,1024]{0,2,1:T(8,128)(2,1)S(1)}, bf16[1024,1,1024]{0,2,1:T(8,128)(2,1)S(1)}) fusion(bf16[1024,3,1024]{0,2,1:T(8,128)(2,1)} %all-gather.3.cloned.1.call-done), kind=kLoop, calls=%fused_computation.88 | loop fusion | bytes 8388608 | tf_op jit(solution)/shard_map/slice | solution.py:192
  114.8 2.4 %fusion.24 = bf16[16,8,8,128]{3,2,1,0:T(8,128)(2,1)S(1)} fusion(bf16[1024,3,1024]{0,2,1:T(8,128)(2,1)} %all-gather.3.cloned.1.call-done, s32[1024]{0:T(1024)S(1)} %bitcast.57, s32[128]{0:T(128)S(1)} %get-tuple-element.17), kind=kOutput, calls=%fused_computation.31 | convolution fusion | flops 268697600 | bytes 2363904 | tf_op jit(solution)/shard_map/dot_general | solution.py:190
  117.2 0.8 multiply_reduce_fusion.1
  118.0 0.9 fusion.2
  118.9 2.9 %fusion.31 = bf16[128,8,128]{0,2,1:T(8,128)(2,1)S(1)} fusion(bf16[1024,8,128]{0,2,1:T(8,128)(2,1)S(1)} %bitcast.49, f32[8,128,1024]{2,1,0:T(8,128)S(1)} %get-tuple-element.11, f32[8,128]{1,0:T(8,128)S(1)} %get-tuple-element.10, f32[128,8]{0,1:T(8,128)S(1)} %bitcast.58), kind=kOutput, calls=%fused_computation.38 | convolution fusion | flops 1612972032 | bytes 6561792 | tf_op jit(solution)/shard_map/hqk,khd->qhd/dot_general | solution.py:233
  121.8 2.2 %multiply_reduce_fusion = (f32[8,128]{1,0:T(8,128)S(1)}, bf16[8,128,1024]{2,1,0:T(8,128)(2,1)S(1)}) fusion(f32[128,1024]{1,0:T(8,128)S(1)} %fusion.33, f32[8,128,1024]{2,1,0:T(8,128)S(1)} %get-tuple-element.11, pred[128,1024]{1,0:T(8,128)(4,1)S(1)} %fusion.34), kind=kOutput, calls=%fused_computation.3 | output fusion | flops 8389631 | bytes 6950912 | tf_op jit(solution)/shard_map/sub | solution.py:218
  124.0 0.8 fusion.9
  124.8 1.0 fusion.29
  125.8 0.4 slice-done.1
  126.2 2.3 %convolution_convert_fusion = bf16[128,4096]{1,0:T(8,128)(2,1)} fusion(bf16[128,1024]{0,1:T(8,128)(2,1)S(1)} %bitcast.53, bf16[1024,4096]{1,0:T(8,128)(2,1)S(1)} %bitcast.48), kind=kOutput, calls=%fused_computation.2 | convolution fusion | flops 1074266112 | bytes 9699328 | tf_op jit(solution)/shard_map/dot_general | solution.py:240
  128.5 0.0 reduce-scatter.2.cloned.1.call-update
  128.5 23.2 %reduce-scatter.2.cloned.1.call-done = bf16[32,4096]{1,0:T(8,128)(2,1)} async-done(((bf16[128,4096]{1,0:T(8,128)(2,1)}), bf16[32,4096]{1,0:T(8,128)(2,1)}) %reduce-scatter.2.cloned.1.call-update) | async-done | bytes 262160 | tf_op jit(solution)/shard_map/reduce_scatter | solution.py:239
  (12 shorter events, 0.1 us)
Async XLA Ops:
  6.5 105.6 %all-gather.3.cloned.1.call-start = ((), (), s32[]{:S(2)}) async-start(), calls=%async_computation.1 | async-start | bytes 7077888 | tf_op jit(solution)/shard_map/all_gather | solution.py:186
  8.9 142.9 %reduce-scatter.2.cloned.1.call-start = ((), (), s32[]{:S(2)}) async-start(), calls=%async_computation.2 | async-start | bytes 1310720 | tf_op jit(solution)/shard_map/reduce_scatter | solution.py:239
  121.8 4.0 %slice-start = ((s8[8388608]{0:T(1024)(128)(4,1)}), s8[4194304]{0:T(1024)(128)(4,1)S(1)}, s32[]{:S(2)}) async-start(s8[8388608]{0:T(1024)(128)(4,1)} %bitcast.47), calls=%async_computation.3 | async-start | bytes 8388608
  124.0 2.2 %slice-start.1 = ((s8[8388608]{0:T(1024)(128)(4,1)}), s8[4194304]{0:T(1024)(128)(4,1)S(1)}, s32[]{:S(2)}) async-start(s8[8388608]{0:T(1024)(128)(4,1)} %bitcast.47), calls=%async_computation.4 | async-start | bytes 8388608
Sparse Core Ops, SparseCore 0:
  9.4 102.6 all-gather.2
  128.6 23.0 reduce-scatter.1
where the time goes:
time: 159 us
  waiting for transfers between devices  98.9 us (62%)
  blocking collectives  22.5 us (14%)
  between operations  14.8 us (9%)
  matrix products  10.2 us (6%)
  local copies, waits for them, and re-layouts  6.94 us (4%)
  other arithmetic  5.17 us (3%)
    all_gather x1, waiting for transfers between devices, gathered_plan(): everything = lax.all_gather(projected, 'seq', tiled=True)  75.7 us
    reduce_scatter x1, waiting for transfers between devices, gathered_plan(): lax.psum_scatter(jnp.dot(attn_rows, out_weight, preferred_element_type=jn...  23.2 us
    all_gather x1, blocking collectives, gathered_plan(): arrival_dest = lax.all_gather(destination, 'seq', tiled=True)  22.5 us
    unnamed x6, local copies, waits for them, and re-layouts  3.44 us
  transfers between devices with their start and end apart: 2, of which 2 were waited for; matrix products, arithmetic and copies ran while one was open for 2% of the time, Pallas kernels for 0%

commit v1 on v0

--- a/solution.py
+++ b/solution.py
@@ -183,7 +183,25 @@
     tokens = owners * tok_dev
     blocks_all = tokens // BLK
     score_scale = 1.0 / math.sqrt(HD)
-    everything = lax.all_gather(projected, "seq", tiled=True)
+    length, position, span = (lax.axis_size("seq"), lax.axis_index("seq"), projected.shape[0])
+    forward = [(i_2, (i_2 + 1) % length) for i_2 in range(length)]
+    left = [(i_2, (i_2 - 1) % length) for i_2 in range(length)]
+    everything = jnp.zeros(
+        (*projected.shape[:0], length * span, *projected.shape[0 + 1 :]), projected.dtype
+    )
+    everything = lax.dynamic_update_slice_in_dim(everything, projected, position * span, axis=0)
+    from_left = from_right = projected
+    half = length // 2
+    for step_2 in range(1, half + 1):
+        from_left = lax.ppermute(from_left, "seq", forward)
+        everything = lax.dynamic_update_slice_in_dim(
+            everything, from_left, (position - step_2) % length * span, axis=0
+        )
+        if step_2 < length - half:
+            from_right = lax.ppermute(from_right, "seq", left)
+            everything = lax.dynamic_update_slice_in_dim(
+                everything, from_right, (position + step_2) % length * span, axis=0
+            )
     arrival_dest = lax.all_gather(destination, "seq", tiled=True)
     my_pos = own_index * tok_dev + jnp.arange(tok_dev, dtype=jnp.int32)
     pick = (arrival_dest[None, :] == my_pos[:, None]).astype(projected.dtype)

time: 159 us -> 187 us (1.18)
  blocking collectives: 22.5 us -> 41.9 us
  starting transfers between devices: 0.04 us -> 18.2 us
  waiting for transfers between devices: 98.9 us -> 91.8 us
    all_gather x1 -> x0, waiting for transfers between devices: 75.7 us -> none  [gathered_plan(): everything = lax.all_gather(projected, 'seq', tiled=True)]
    ppermute x0 -> x7, waiting for transfers between devices: none -> 69.5 us  [the longest x4 69.5 us: gathered_plan(): from_left = lax.ppermute(from_left, 'seq', forward)]
    all_gather x1, blocking collectives: 22.5 us -> 41.9 us  [gathered_plan(): arrival_dest = lax.all_gather(destination, 'seq', tiled=True)]
    ppermute x0 -> x7, starting transfers between devices: none -> 18.2 us  [the longest x3 10.2 us: gathered_plan(): from_right = lax.ppermute(from_right, 'seq', left)]
    slice x1, local copies, waits for them, and re-layouts: 2.66 us -> 0.44 us  [gathered_plan(): keys = everything[:, 1, :].reshape(tokens, heads_here, HD)]
    dynamic_update_slice x0 -> x8, local copies, waits for them, and re-layouts: none -> 2.18 us  [the longest x4 1.08 us: gathered_plan(): lax.dynamic_update_slice_in_dim(everything, from_left, (position - step_2...]
  transfers between devices with their start and end apart: 2 -> 8, of which waited for: 2 -> 4; matrix products, arithmetic and copies ran while one was open for 2% -> 3% of each run, Pallas kernels for 0% -> 0%
where the time goes in v1:
time: 187 us
  waiting for transfers between devices  91.8 us (49%)
  blocking collectives  41.9 us (22%)
  starting transfers between devices  18.2 us (10%)
  between operations  14.9 us (8%)
  matrix products  8.34 us (4%)
  local copies, waits for them, and re-layouts  6.55 us (4%)
  other arithmetic  5.08 us (3%)
    ppermute x4, waiting for transfers between devices, gathered_plan(): from_left = lax.ppermute(from_left, 'seq', forward)  69.5 us
    all_gather x1, blocking collectives, gathered_plan(): arrival_dest = lax.all_gather(destination, 'seq', tiled=True)  41.9 us
    reduce_scatter x1, waiting for transfers between devices, gathered_plan(): lax.psum_scatter(jnp.dot(attn_rows, out_weight, preferred_element_type=jn...  22.3 us
    ppermute x3, starting transfers between devices, gathered_plan(): from_right = lax.ppermute(from_right, 'seq', left)  10.2 us
    ppermute x4, starting transfers between devices, gathered_plan(): from_left = lax.ppermute(from_left, 'seq', forward)  8.04 us
  transfers between devices with their start and end apart: 8, of which 4 were waited for; matrix products, arithmetic and copies ran while one was open for 3% of the time, Pallas kernels for 0%

profile of v1, /device:TPU:0, one launch (start us, length us, event | category | flops | bytes accessed | tf_op | source)
XLA Modules:
  0.0 186.8 jit_solution(12190818843260191830)
XLA Ops:
  6.5 1.5 copy.29
  8.1 3.0 %collective-permute-start = (bf16[128,3,1024]{0,2,1:T(8,128)(2,1)S(1)}, bf16[128,3,1024]{0,2,1:T(8,128)(2,1)S(1)}, u32[]{:S(2)}, u32[]{:S(2)}) collective-permute-start(bf16[128,3,1024]{0,2,1:T(8,128)(2,1)S(1)} %copy.29), channel_id=1, source_target_pairs={{0,4},{4,8},{8,12},{12,16},{16,20},{20,24},{24,28},{28,0},{1,5},{5... | collective-permute-start | bytes 2359304 | tf_op jit(solution)/shard_map/ppermute | solution.py:196
  11.1 3.1 %collective-permute-start.1 = (bf16[128,3,1024]{0,2,1:T(8,128)(2,1)S(1)}, bf16[128,3,1024]{0,2,1:T(8,128)(2,1)S(1)}, u32[]{:S(2)}, u32[]{:S(2)}) collective-permute-start(bf16[128,3,1024]{0,2,1:T(8,128)(2,1)S(1)} %copy.29), channel_id=1, source_target_pairs={{0,28},{4,0},{8,4},{12,8},{16,12},{20,16},{24,20},{28,24},{1,29},{... | collective-permute-start | bytes 2359304 | tf_op jit(solution)/shard_map/ppermute | solution.py:201
  15.5 0.8 copy.34
  16.3 0.8 reduce-window.8
  17.1 0.6 gather_fusion
  17.8 41.9 %all-gather = s32[8,1,128]{2,1,0:T(1,128)S(1)} all-gather(s32[1,1,128]{2,1,0:T(1,128)} %bitcast.59), channel_id=1, replica_groups=mesh['seq'=8,'head'=4] {'seq'}, dimensions={0}, use_global_device_ids=true | all-gather | bytes 4608 | tf_op jit(solution)/shard_map/all_gather | solution.py:205
  60.1 4.8 %collective-permute-start.3 = (bf16[128,3,1024]{0,2,1:T(8,128)(2,1)S(1)}, bf16[128,3,1024]{0,2,1:T(8,128)(2,1)S(1)}, u32[]{:S(2)}, u32[]{:S(2)}) collective-permute-start(bf16[128,3,1024]{0,2,1:T(8,128)(2,1)S(1)} %collective-permute-done.1), channel_id=1, source_target_pairs={{0,28},{4,0},{8,4},{12,8},{16,12},{20,16},{24,20},{28,24},{1,29},{... | collective-permute-start | bytes 2359304 | tf_op jit(solution)/shard_map/ppermute | solution.py:201
  64.9 25.2 %collective-permute-done.2 = bf16[128,3,1024]{0,2,1:T(8,128)(2,1)S(1)} collective-permute-done((bf16[128,3,1024]{0,2,1:T(8,128)(2,1)S(1)}, bf16[128,3,1024]{0,2,1:T(8,128)(2,1)S(1)}, u32[]{:S(2)}, u32[]{:S(2)}) %collective-permute-start.2) | collective-permute-done | bytes 786464 | tf_op jit(solution)/shard_map/ppermute | solution.py:196
  90.1 2.5 %collective-permute-start.4 = (bf16[128,3,1024]{0,2,1:T(8,128)(2,1)S(1)}, bf16[128,3,1024]{0,2,1:T(8,128)(2,1)S(1)}, u32[]{:S(2)}, u32[]{:S(2)}) collective-permute-start(bf16[128,3,1024]{0,2,1:T(8,128)(2,1)S(1)} %collective-permute-done.2), channel_id=1, source_target_pairs={{0,4},{4,8},{8,12},{12,16},{16,20},{20,24},{24,28},{28,0},{1,5},{5... | collective-permute-start | bytes 2359304 | tf_op jit(solution)/shard_map/ppermute | solution.py:196
  93.6 2.3 %collective-permute-start.5 = (bf16[128,3,1024]{0,2,1:T(8,128)(2,1)S(1)}, bf16[128,3,1024]{0,2,1:T(8,128)(2,1)S(1)}, u32[]{:S(2)}, u32[]{:S(2)}) collective-permute-start(bf16[128,3,1024]{0,2,1:T(8,128)(2,1)S(1)} %collective-permute-done.3), channel_id=1, source_target_pairs={{0,28},{4,0},{8,4},{12,8},{16,12},{20,16},{24,20},{28,24},{1,29},{... | collective-permute-start | bytes 2359304 | tf_op jit(solution)/shard_map/ppermute | solution.py:201
  95.9 0.8 broadcast_in_dim.13
  97.0 28.3 %collective-permute-done.4 = bf16[128,3,1024]{0,2,1:T(8,128)(2,1)S(1)} collective-permute-done((bf16[128,3,1024]{0,2,1:T(8,128)(2,1)S(1)}, bf16[128,3,1024]{0,2,1:T(8,128)(2,1)S(1)}, u32[]{:S(2)}, u32[]{:S(2)}) %collective-permute-start.4) | collective-permute-done | bytes 786464 | tf_op jit(solution)/shard_map/ppermute | solution.py:196
  125.3 2.5 %collective-permute-start.6 = (bf16[128,3,1024]{0,2,1:T(8,128)(2,1)S(1)}, bf16[128,3,1024]{0,2,1:T(8,128)(2,1)S(1)}, u32[]{:S(2)}, u32[]{:S(2)}) collective-permute-start(bf16[128,3,1024]{0,2,1:T(8,128)(2,1)S(1)} %collective-permute-done.4), channel_id=1, source_target_pairs={{0,4},{4,8},{8,12},{12,16},{16,20},{20,24},{24,28},{28,0},{1,5},{5... | collective-permute-start | bytes 2359304 | tf_op jit(solution)/shard_map/ppermute | solution.py:196
  129.5 16.0 %collective-permute-done.6 = bf16[128,3,1024]{0,2,1:T(8,128)(2,1)S(1)} collective-permute-done((bf16[128,3,1024]{0,2,1:T(8,128)(2,1)S(1)}, bf16[128,3,1024]{0,2,1:T(8,128)(2,1)S(1)}, u32[]{:S(2)}, u32[]{:S(2)}) %collective-permute-start.6) | collective-permute-done | bytes 786464 | tf_op jit(solution)/shard_map/ppermute | solution.py:196
  146.2 0.8 fusion.28
  147.1 0.8 multiply_reduce_fusion.1
  147.8 0.9 fusion.2
  148.7 2.1 %multiply_reduce_fusion = (f32[8,128]{1,0:T(8,128)S(1)}, bf16[8,128,1024]{2,1,0:T(8,128)(2,1)S(1)}) fusion(f32[128,1024]{1,0:T(8,128)S(1)} %fusion.43, f32[8,128,1024]{2,1,0:T(8,128)S(1)} %get-tuple-element.11, pred[128,1024]{1,0:T(8,128)(4,1)S(1)} %fusion.44), kind=kOutput, calls=%fused_computation.3 | output fusion | flops 8389631 | bytes 6950912 | tf_op jit(solution)/shard_map/sub | solution.py:236
  150.9 0.7 fusion.11
  151.6 2.8 %fusion.41 = bf16[128,8,128]{0,2,1:T(8,128)(2,1)S(1)} fusion(bf16[1024,8,128]{0,2,1:T(8,128)(2,1)S(1)} %bitcast.51, f32[8,128,1024]{2,1,0:T(8,128)S(1)} %get-tuple-element.11, f32[8,128]{1,0:T(8,128)S(1)} %get-tuple-element.10, f32[128,8]{0,1:T(8,128)S(1)} %bitcast.58), kind=kOutput, calls=%fused_computation.38 | convolution fusion | flops 1612972032 | bytes 6561792 | tf_op jit(solution)/shard_map/hqk,khd->qhd/dot_general | solution.py:251
  154.4 0.9 fusion.35
  155.4 2.3 %convolution_convert_fusion = bf16[128,4096]{1,0:T(8,128)(2,1)} fusion(bf16[128,1024]{0,1:T(8,128)(2,1)S(1)} %bitcast.53, bf16[1024,4096]{1,0:T(8,128)(2,1)S(1)} %bitcast.48), kind=kOutput, calls=%fused_computation.2 | convolution fusion | flops 1074266112 | bytes 9699328 | tf_op jit(solution)/shard_map/dot_general | solution.py:258
  157.7 22.3 %reduce-scatter.2.cloned.1.call-done = bf16[32,4096]{1,0:T(8,128)(2,1)} async-done(((bf16[128,4096]{1,0:T(8,128)(2,1)}), bf16[32,4096]{1,0:T(8,128)(2,1)}) %reduce-scatter.2.cloned.1.call-update) | async-done | bytes 262160 | tf_op jit(solution)/shard_map/reduce_scatter | solution.py:257
  (33 shorter events, 4.2 us)
Async XLA Ops:
  6.5 173.4 %reduce-scatter.2.cloned.1.call-start = ((), (), s32[]{:S(2)}) async-start(), calls=%async_computation.1 | async-start | bytes 1310720 | tf_op jit(solution)/shard_map/reduce_scatter | solution.py:257
  8.1 51.6 %collective-permute-start = (bf16[128,3,1024]{0,2,1:T(8,128)(2,1)S(1)}, bf16[128,3,1024]{0,2,1:T(8,128)(2,1)S(1)}, u32[]{:S(2)}, u32[]{:S(2)}) collective-permute-start(bf16[128,3,1024]{0,2,1:T(8,128)(2,1)S(1)} %copy.29), channel_id=1, source_target_pairs={{0,4},{4,8},{8,12},{12,16},{16,20},{20,24},{24,28},{28,0},{1,5},{5... | collective-permute-start | bytes 2359304 | tf_op jit(solution)/shard_map/ppermute | solution.py:196
  11.1 49.0 %collective-permute-start.1 = (bf16[128,3,1024]{0,2,1:T(8,128)(2,1)S(1)}, bf16[128,3,1024]{0,2,1:T(8,128)(2,1)S(1)}, u32[]{:S(2)}, u32[]{:S(2)}) collective-permute-start(bf16[128,3,1024]{0,2,1:T(8,128)(2,1)S(1)} %copy.29), channel_id=1, source_target_pairs={{0,28},{4,0},{8,4},{12,8},{16,12},{20,16},{24,20},{28,24},{1,29},{... | collective-permute-start | bytes 2359304 | tf_op jit(solution)/shard_map/ppermute | solution.py:201
  59.6 30.4 %collective-permute-start.2 = (bf16[128,3,1024]{0,2,1:T(8,128)(2,1)S(1)}, bf16[128,3,1024]{0,2,1:T(8,128)(2,1)S(1)}, u32[]{:S(2)}, u32[]{:S(2)}) collective-permute-start(bf16[128,3,1024]{0,2,1:T(8,128)(2,1)S(1)} %collective-permute-done), channel_id=1, source_target_pairs={{0,4},{4,8},{8,12},{12,16},{16,20},{20,24},{24,28},{28,0},{1,5},{5... | collective-permute-start | bytes 2359304 | tf_op jit(solution)/shard_map/ppermute | solution.py:196
  60.1 33.5 %collective-permute-start.3 = (bf16[128,3,1024]{0,2,1:T(8,128)(2,1)S(1)}, bf16[128,3,1024]{0,2,1:T(8,128)(2,1)S(1)}, u32[]{:S(2)}, u32[]{:S(2)}) collective-permute-start(bf16[128,3,1024]{0,2,1:T(8,128)(2,1)S(1)} %collective-permute-done.1), channel_id=1, source_target_pairs={{0,28},{4,0},{8,4},{12,8},{16,12},{20,16},{24,20},{28,24},{1,29},{... | collective-permute-start | bytes 2359304 | tf_op jit(solution)/shard_map/ppermute | solution.py:201
  90.1 35.2 %collective-permute-start.4 = (bf16[128,3,1024]{0,2,1:T(8,128)(2,1)S(1)}, bf16[128,3,1024]{0,2,1:T(8,128)(2,1)S(1)}, u32[]{:S(2)}, u32[]{:S(2)}) collective-permute-start(bf16[128,3,1024]{0,2,1:T(8,128)(2,1)S(1)} %collective-permute-done.2), channel_id=1, source_target_pairs={{0,4},{4,8},{8,12},{12,16},{16,20},{20,24},{24,28},{28,0},{1,5},{5... | collective-permute-start | bytes 2359304 | tf_op jit(solution)/shard_map/ppermute | solution.py:196
  93.6 35.6 %collective-permute-start.5 = (bf16[128,3,1024]{0,2,1:T(8,128)(2,1)S(1)}, bf16[128,3,1024]{0,2,1:T(8,128)(2,1)S(1)}, u32[]{:S(2)}, u32[]{:S(2)}) collective-permute-start(bf16[128,3,1024]{0,2,1:T(8,128)(2,1)S(1)} %collective-permute-done.3), channel_id=1, source_target_pairs={{0,28},{4,0},{8,4},{12,8},{16,12},{20,16},{24,20},{28,24},{1,29},{... | collective-permute-start | bytes 2359304 | tf_op jit(solution)/shard_map/ppermute | solution.py:201
  125.3 20.2 %collective-permute-start.6 = (bf16[128,3,1024]{0,2,1:T(8,128)(2,1)S(1)}, bf16[128,3,1024]{0,2,1:T(8,128)(2,1)S(1)}, u32[]{:S(2)}, u32[]{:S(2)}) collective-permute-start(bf16[128,3,1024]{0,2,1:T(8,128)(2,1)S(1)} %collective-permute-done.4), channel_id=1, source_target_pairs={{0,4},{4,8},{8,12},{12,16},{16,20},{20,24},{24,28},{28,0},{1,5},{5... | collective-permute-start | bytes 2359304 | tf_op jit(solution)/shard_map/ppermute | solution.py:196
  150.8 4.5 %slice-start = ((s8[8388608]{0:T(1024)(128)(4,1)}), s8[4194304]{0:T(1024)(128)(4,1)S(1)}, s32[]{:S(2)}) async-start(s8[8388608]{0:T(1024)(128)(4,1)} %bitcast.47), calls=%async_computation.2 | async-start | bytes 8388608
  151.6 3.8 %slice-start.1 = ((s8[8388608]{0:T(1024)(128)(4,1)}), s8[4194304]{0:T(1024)(128)(4,1)S(1)}, s32[]{:S(2)}) async-start(s8[8388608]{0:T(1024)(128)(4,1)} %bitcast.47), calls=%async_computation.3 | async-start | bytes 8388608
Sparse Core Ops, SparseCore 0:
  157.8 22.1 reduce-scatter.1
